TPU v7x, 32 devices: a whole 2x2x4 slice. The times are simulated.
32 devices in a mesh: ctx: 8 (over z, y), tp: 4 (over x, core).
Axes of the slice: x: 2, y: 2, z: 4, core: 2. Of those that a mesh axis runs over, the one named last changes fastest.
Arguments:
- queries: bfloat16 [2048, 16, 128], P('ctx', 'tp'), may hold values from -12 to 12
- keys: bfloat16 [2048, 8, 128], P('ctx', 'tp'), may hold values from -6 to 6
- values: bfloat16 [2048, 8, 128], P('ctx', 'tp'), may hold values from -6 to 6
- residual: bfloat16 [2048, 3072], P('ctx', 'tp'), may hold values from -6 to 6
- out_weight: bfloat16 [16, 128, 3072], P(None, None, 'tp'), may hold values from -1 to 1
- post_gain: bfloat16 [3072], P('tp'), may hold values from 0.099609375 to 1.8984375
Outputs:
- mixed: bfloat16 [2048, 3072], P('ctx', 'tp')
All inputs are finite; a program needn't handle non-finite values.
Results may differ from a plain program's by a relative error of at most 0.015.
Values may be sent and summed in bfloat16 or wider, within the bound.
No kernel may reach another device: no remote copies, remote signals or barrier semaphores. Data moves between devices by JAX's collectives and lax.ppermute only.
A program may use at most 64 MiB of HBM per device.

v0:
```python
import jax
import jax.numpy as jnp
from jax import lax
from jax.sharding import PartitionSpec as P

WINDOW_TOKENS = 4096
D = 3072
softcap_value = 50.0
query_scale = 1.0 / 12.0
rope_base = 10000.0


def passed_along(value, axis, steps):
    count = lax.axis_size(axis)
    first, last = (max(0, -steps), min(count, count - steps))
    return lax.ppermute(value, axis, [(source, source + steps) for source in range(first, last)])


def rotate(values_in, positions):
    half_width = values_in.shape[-1] // 2
    steps_half = jnp.arange(half_width, dtype=jnp.float32)
    inverse = rope_base ** (-2.0 * steps_half / values_in.shape[-1])
    angles = positions.astype(jnp.float32)[..., None] * inverse
    cosine = jnp.cos(angles)
    sine_part = jnp.sin(angles)
    first_half = values_in[..., :half_width]
    second_half = values_in[..., half_width:]
    return jnp.concatenate(
        [
            first_half * cosine - second_half * sine_part,
            second_half * cosine + first_half * sine_part,
        ],
        axis=-1,
    )


def attend_block(state, key_block, value_block, source, rotary_queries, device_index):
    numerators, denominators = state
    rows = key_block.shape[0]
    scores = (
        jnp.einsum("sgrh,kgh->grsk", rotary_queries, key_block, preferred_element_type=jnp.float32)
        * query_scale
    )
    capped = softcap_value * jnp.tanh(scores / softcap_value)
    offsets = jnp.arange(rows, dtype=jnp.int32)
    query_pos = device_index * rows + offsets
    key_pos = source * rows + offsets
    distance = query_pos[:, None] - key_pos[None, :]
    allowed = (distance >= 0) & (distance < WINDOW_TOKENS) & (key_pos[None, :] >= 0)
    weights = jnp.where(allowed[None, None], jnp.exp(capped), 0.0)
    denominators = denominators + jnp.sum(weights, axis=-1)
    numerators = numerators + jnp.einsum(
        "grsk,kgh->grsh",
        weights.astype(jnp.bfloat16),
        value_block,
        preferred_element_type=jnp.float32,
    )
    return (numerators, denominators)


def local(queries, keys, values, residual, out_weight, post_gain):
    rows = queries.shape[0]
    q_heads = queries.shape[1]
    head_size = queries.shape[2]
    kv_heads = keys.shape[1]
    heads_per_group = q_heads // kv_heads
    cycle_size = lax.axis_size("ctx")
    device_index = lax.axis_index("ctx")
    positions = (device_index * rows + jnp.arange(rows, dtype=jnp.int32))[:, None]
    rotary_queries = rotate(queries.astype(jnp.float32), positions).astype(jnp.bfloat16)
    rotary_queries = rotary_queries.reshape(rows, kv_heads, heads_per_group, head_size)
    rotary_keys = rotate(keys.astype(jnp.float32), positions).astype(jnp.bfloat16)
    reach = min(WINDOW_TOKENS // rows, cycle_size - 1)
    state = (
        jnp.zeros((kv_heads, heads_per_group, rows, head_size), jnp.float32),
        jnp.zeros((kv_heads, heads_per_group, rows), jnp.float32),
    )
    state = attend_block(state, rotary_keys, values, device_index, rotary_queries, device_index)

    def advance(step_index, carried):
        running, key_block, value_block = carried
        key_block, value_block = passed_along((key_block, value_block), "ctx", 1)
        running = attend_block(
            running,
            key_block,
            value_block,
            device_index - step_index - 1,
            rotary_queries,
            device_index,
        )
        return (running, key_block, value_block)

    state, unused_keys, unused_values = lax.fori_loop(
        0, reach, advance, (state, rotary_keys, values)
    )
    numerators, denominators = state
    attended = (numerators / denominators[..., None]).astype(jnp.bfloat16)
    attended = jnp.transpose(attended, (2, 0, 1, 3)).reshape(rows, q_heads, head_size)
    local_cols = out_weight.shape[2]
    piece = lax.all_gather(attended, "tp", axis=1, tiled=True)
    heads_in = piece.shape[1]
    weight_rows = out_weight.reshape(heads_in * head_size, local_cols)
    projected = jnp.dot(
        piece.reshape(rows, heads_in * head_size), weight_rows, preferred_element_type=jnp.float32
    )
    square_sums = lax.psum(jnp.sum(projected * projected, axis=1), "tp")
    normed = projected * lax.rsqrt(square_sums / D + 1e-06)[:, None] * post_gain.astype(jnp.float32)
    mixed = residual.astype(jnp.float32) + normed
    return mixed.astype(jnp.bfloat16)


def solution(mesh):
    in_specs = (
        P("ctx", "tp", None),
        P("ctx", "tp", None),
        P("ctx", "tp", None),
        P("ctx", "tp"),
        P(None, None, "tp"),
        P("tp"),
    )
    out_specs = P("ctx", "tp")
    return jax.shard_map(local, mesh=mesh, in_specs=in_specs, out_specs=out_specs, check_vma=False)
```

profile of v0, /device:TPU:0, one launch (start us, length us, event | category | flops | bytes accessed | tf_op | source)
XLA Modules:
  0.0 137.2 jit_solution(11933492602181658960)
XLA Ops:
  6.6 1.1 copy_convert_fusion
  7.7 1.0 convert_element_type.47
  8.7 0.5 multiply_cosine_fusion
  9.2 0.8 subtract_convert_fusion.1
  10.1 0.5 subtract_convert_fusion
  10.6 0.7 copy.17
  11.4 0.7 copy.20
  12.1 1.1 pad_maximum_fusion.1
  13.1 1.1 pad_maximum_fusion
  14.5 0.5 fusion.24
  15.0 1.2 fusion.15
  16.1 85.1 %while.21 = (s32[]{:T(128)}, f32[2,2,256,128]{3,2,1,0:T(8,128)}, f32[2,2,256]{2,1,0:T(2,128)S(1)}, bf16[256,2,128]{2,0,1:T(8,128)(2,1)}, bf16[256,2,128]{2,0,1:T...) while((s32[]{:T(128)}, f32[2,2,256,128]{3,2,1,0:T(8,128)}, ...), condition=%wide.region_3.4_spmd, body=%wide.region_1.3_spmd.sunk | while | flops 135988224 | bytes 8540965 | solution.py:93
  16.1 4.9 %collective-permute-start = (bf16[256,2,128]{2,0,1:T(8,128)(2,1)}, bf16[256,2,128]{2,0,1:T(8,128)(2,1)S(1)}, u32[]{:S(2)}, u32[]{:S(2)}) collective-permute-start(bf16[256,2,128]{2,0,1:T(8,128)(2,1)} %get-tuple-element.308), channel_id=1, source_target_pairs={{0,4},{4,8},{8,12},{12,16},{16,20},{20,24},{24,28},{1,5},{5,9},{9,... | collective-permute-start | bytes 393224 | tf_op jit(solution)/shard_map/while/body/eval_jaxpr/ppermute | solution.py:16
  21.0 3.4 %collective-permute-start.1 = (bf16[256,2,128]{2,0,1:T(8,128)(2,1)S(1)}, bf16[256,2,128]{2,0,1:T(8,128)(2,1)S(1)}, u32[]{:S(2)}, u32[]{:S(2)}) collective-permute-start(bf16[256,2,128]{2,0,1:T(8,128)(2,1)S(1)} %get-tuple-element.309), channel_id=1, source_target_pairs={{0,4},{4,8},{8,12},{12,16},{16,20},{20,24},{24,28},{1,5},{5,9},{9,... | collective-permute-start | bytes 393224 | tf_op jit(solution)/shard_map/while/body/eval_jaxpr/ppermute | solution.py:16
  24.7 1.4 %fusion.40 = (f32[2,2,256]{2,1,0:T(2,128)S(1)}, bf16[2,2,256,256]{2,3,1,0:T(8,128)(2,1)S(1)}) fusion(bf16[256,2,2,128]{3,0,2,1:T(8,128)(2,1)} %get-tuple-element.323, bf16[256,2,128]{2,0,1:T(8,128)(2,1)S(1)} %collective-permute-done, pred[256,256]{0,1:T(8,128)(4,1)S(1)} %fusion.39), kind=kOutput, calls=%fused_computation.49.clone.1 | convolution fusion | flops 68418560 | bytes 987136 | tf_op jit(solution)/shard_map/while/body/eval_jaxpr/sgrh,kgh->grsk/dot_general | solution.py:41
  26.1 0.6 copy.45
  27.0 0.4 convolution_add_fusion.2
  27.4 0.8 copy-done.2
  28.2 4.3 %collective-permute-start = (bf16[256,2,128]{2,0,1:T(8,128)(2,1)}, bf16[256,2,128]{2,0,1:T(8,128)(2,1)S(1)}, u32[]{:S(2)}, u32[]{:S(2)}) collective-permute-start(bf16[256,2,128]{2,0,1:T(8,128)(2,1)} %get-tuple-element.308), channel_id=1, source_target_pairs={{0,4},{4,8},{8,12},{12,16},{16,20},{20,24},{24,28},{1,5},{5,9},{9,... | collective-permute-start | bytes 393224 | tf_op jit(solution)/shard_map/while/body/eval_jaxpr/ppermute | solution.py:16
  32.5 4.3 %collective-permute-start.1 = (bf16[256,2,128]{2,0,1:T(8,128)(2,1)S(1)}, bf16[256,2,128]{2,0,1:T(8,128)(2,1)S(1)}, u32[]{:S(2)}, u32[]{:S(2)}) collective-permute-start(bf16[256,2,128]{2,0,1:T(8,128)(2,1)S(1)} %get-tuple-element.309), channel_id=1, source_target_pairs={{0,4},{4,8},{8,12},{12,16},{16,20},{20,24},{24,28},{1,5},{5,9},{9,... | collective-permute-start | bytes 393224 | tf_op jit(solution)/shard_map/while/body/eval_jaxpr/ppermute | solution.py:16
  37.1 1.4 %fusion.40 = (f32[2,2,256]{2,1,0:T(2,128)S(1)}, bf16[2,2,256,256]{2,3,1,0:T(8,128)(2,1)S(1)}) fusion(bf16[256,2,2,128]{3,0,2,1:T(8,128)(2,1)} %get-tuple-element.323, bf16[256,2,128]{2,0,1:T(8,128)(2,1)S(1)} %collective-permute-done, pred[256,256]{0,1:T(8,128)(4,1)S(1)} %fusion.39), kind=kOutput, calls=%fused_computation.49.clone.1 | convolution fusion | flops 68418560 | bytes 987136 | tf_op jit(solution)/shard_map/while/body/eval_jaxpr/sgrh,kgh->grsk/dot_general | solution.py:41
  38.5 0.6 copy.45
  39.2 0.2 collective-permute-done.1
  39.4 0.4 convolution_add_fusion.2
  39.8 0.8 copy-done.2
  40.6 4.3 %collective-permute-start = (bf16[256,2,128]{2,0,1:T(8,128)(2,1)}, bf16[256,2,128]{2,0,1:T(8,128)(2,1)S(1)}, u32[]{:S(2)}, u32[]{:S(2)}) collective-permute-start(bf16[256,2,128]{2,0,1:T(8,128)(2,1)} %get-tuple-element.308), channel_id=1, source_target_pairs={{0,4},{4,8},{8,12},{12,16},{16,20},{20,24},{24,28},{1,5},{5,9},{9,... | collective-permute-start | bytes 393224 | tf_op jit(solution)/shard_map/while/body/eval_jaxpr/ppermute | solution.py:16
  45.0 4.1 %collective-permute-start.1 = (bf16[256,2,128]{2,0,1:T(8,128)(2,1)S(1)}, bf16[256,2,128]{2,0,1:T(8,128)(2,1)S(1)}, u32[]{:S(2)}, u32[]{:S(2)}) collective-permute-start(bf16[256,2,128]{2,0,1:T(8,128)(2,1)S(1)} %get-tuple-element.309), channel_id=1, source_target_pairs={{0,4},{4,8},{8,12},{12,16},{16,20},{20,24},{24,28},{1,5},{5,9},{9,... | collective-permute-start | bytes 393224 | tf_op jit(solution)/shard_map/while/body/eval_jaxpr/ppermute | solution.py:16
  49.3 1.4 %fusion.40 = (f32[2,2,256]{2,1,0:T(2,128)S(1)}, bf16[2,2,256,256]{2,3,1,0:T(8,128)(2,1)S(1)}) fusion(bf16[256,2,2,128]{3,0,2,1:T(8,128)(2,1)} %get-tuple-element.323, bf16[256,2,128]{2,0,1:T(8,128)(2,1)S(1)} %collective-permute-done, pred[256,256]{0,1:T(8,128)(4,1)S(1)} %fusion.39), kind=kOutput, calls=%fused_computation.49.clone.1 | convolution fusion | flops 68418560 | bytes 987136 | tf_op jit(solution)/shard_map/while/body/eval_jaxpr/sgrh,kgh->grsk/dot_general | solution.py:41
  50.8 0.6 copy.45
  51.4 0.2 collective-permute-done.1
  51.6 0.4 convolution_add_fusion.2
  52.0 0.8 copy-done.2
  52.8 4.4 %collective-permute-start = (bf16[256,2,128]{2,0,1:T(8,128)(2,1)}, bf16[256,2,128]{2,0,1:T(8,128)(2,1)S(1)}, u32[]{:S(2)}, u32[]{:S(2)}) collective-permute-start(bf16[256,2,128]{2,0,1:T(8,128)(2,1)} %get-tuple-element.308), channel_id=1, source_target_pairs={{0,4},{4,8},{8,12},{12,16},{16,20},{20,24},{24,28},{1,5},{5,9},{9,... | collective-permute-start | bytes 393224 | tf_op jit(solution)/shard_map/while/body/eval_jaxpr/ppermute | solution.py:16
  57.2 3.7 %collective-permute-start.1 = (bf16[256,2,128]{2,0,1:T(8,128)(2,1)S(1)}, bf16[256,2,128]{2,0,1:T(8,128)(2,1)S(1)}, u32[]{:S(2)}, u32[]{:S(2)}) collective-permute-start(bf16[256,2,128]{2,0,1:T(8,128)(2,1)S(1)} %get-tuple-element.309), channel_id=1, source_target_pairs={{0,4},{4,8},{8,12},{12,16},{16,20},{20,24},{24,28},{1,5},{5,9},{9,... | collective-permute-start | bytes 393224 | tf_op jit(solution)/shard_map/while/body/eval_jaxpr/ppermute | solution.py:16
  61.1 1.4 %fusion.40 = (f32[2,2,256]{2,1,0:T(2,128)S(1)}, bf16[2,2,256,256]{2,3,1,0:T(8,128)(2,1)S(1)}) fusion(bf16[256,2,2,128]{3,0,2,1:T(8,128)(2,1)} %get-tuple-element.323, bf16[256,2,128]{2,0,1:T(8,128)(2,1)S(1)} %collective-permute-done, pred[256,256]{0,1:T(8,128)(4,1)S(1)} %fusion.39), kind=kOutput, calls=%fused_computation.49.clone.1 | convolution fusion | flops 68418560 | bytes 987136 | tf_op jit(solution)/shard_map/while/body/eval_jaxpr/sgrh,kgh->grsk/dot_general | solution.py:41
  62.5 0.6 copy.45
  63.4 0.4 convolution_add_fusion.2
  63.8 0.8 copy-done.2
  64.6 4.3 %collective-permute-start = (bf16[256,2,128]{2,0,1:T(8,128)(2,1)}, bf16[256,2,128]{2,0,1:T(8,128)(2,1)S(1)}, u32[]{:S(2)}, u32[]{:S(2)}) collective-permute-start(bf16[256,2,128]{2,0,1:T(8,128)(2,1)} %get-tuple-element.308), channel_id=1, source_target_pairs={{0,4},{4,8},{8,12},{12,16},{16,20},{20,24},{24,28},{1,5},{5,9},{9,... | collective-permute-start | bytes 393224 | tf_op jit(solution)/shard_map/while/body/eval_jaxpr/ppermute | solution.py:16
  69.0 4.1 %collective-permute-start.1 = (bf16[256,2,128]{2,0,1:T(8,128)(2,1)S(1)}, bf16[256,2,128]{2,0,1:T(8,128)(2,1)S(1)}, u32[]{:S(2)}, u32[]{:S(2)}) collective-permute-start(bf16[256,2,128]{2,0,1:T(8,128)(2,1)S(1)} %get-tuple-element.309), channel_id=1, source_target_pairs={{0,4},{4,8},{8,12},{12,16},{16,20},{20,24},{24,28},{1,5},{5,9},{9,... | collective-permute-start | bytes 393224 | tf_op jit(solution)/shard_map/while/body/eval_jaxpr/ppermute | solution.py:16
  73.3 1.4 %fusion.40 = (f32[2,2,256]{2,1,0:T(2,128)S(1)}, bf16[2,2,256,256]{2,3,1,0:T(8,128)(2,1)S(1)}) fusion(bf16[256,2,2,128]{3,0,2,1:T(8,128)(2,1)} %get-tuple-element.323, bf16[256,2,128]{2,0,1:T(8,128)(2,1)S(1)} %collective-permute-done, pred[256,256]{0,1:T(8,128)(4,1)S(1)} %fusion.39), kind=kOutput, calls=%fused_computation.49.clone.1 | convolution fusion | flops 68418560 | bytes 987136 | tf_op jit(solution)/shard_map/while/body/eval_jaxpr/sgrh,kgh->grsk/dot_general | solution.py:41
  74.7 0.6 copy.45
  75.4 0.2 collective-permute-done.1
  75.6 0.4 convolution_add_fusion.2
  76.0 0.8 copy-done.2
  76.8 4.3 %collective-permute-start = (bf16[256,2,128]{2,0,1:T(8,128)(2,1)}, bf16[256,2,128]{2,0,1:T(8,128)(2,1)S(1)}, u32[]{:S(2)}, u32[]{:S(2)}) collective-permute-start(bf16[256,2,128]{2,0,1:T(8,128)(2,1)} %get-tuple-element.308), channel_id=1, source_target_pairs={{0,4},{4,8},{8,12},{12,16},{16,20},{20,24},{24,28},{1,5},{5,9},{9,... | collective-permute-start | bytes 393224 | tf_op jit(solution)/shard_map/while/body/eval_jaxpr/ppermute | solution.py:16
  81.1 3.7 %collective-permute-start.1 = (bf16[256,2,128]{2,0,1:T(8,128)(2,1)S(1)}, bf16[256,2,128]{2,0,1:T(8,128)(2,1)S(1)}, u32[]{:S(2)}, u32[]{:S(2)}) collective-permute-start(bf16[256,2,128]{2,0,1:T(8,128)(2,1)S(1)} %get-tuple-element.309), channel_id=1, source_target_pairs={{0,4},{4,8},{8,12},{12,16},{16,20},{20,24},{24,28},{1,5},{5,9},{9,... | collective-permute-start | bytes 393224 | tf_op jit(solution)/shard_map/while/body/eval_jaxpr/ppermute | solution.py:16
  85.0 1.4 %fusion.40 = (f32[2,2,256]{2,1,0:T(2,128)S(1)}, bf16[2,2,256,256]{2,3,1,0:T(8,128)(2,1)S(1)}) fusion(bf16[256,2,2,128]{3,0,2,1:T(8,128)(2,1)} %get-tuple-element.323, bf16[256,2,128]{2,0,1:T(8,128)(2,1)S(1)} %collective-permute-done, pred[256,256]{0,1:T(8,128)(4,1)S(1)} %fusion.39), kind=kOutput, calls=%fused_computation.49.clone.1 | convolution fusion | flops 68418560 | bytes 987136 | tf_op jit(solution)/shard_map/while/body/eval_jaxpr/sgrh,kgh->grsk/dot_general | solution.py:41
  86.5 0.6 copy.45
  87.3 0.4 convolution_add_fusion.2
  87.8 0.8 copy-done.2
  88.6 4.3 %collective-permute-start = (bf16[256,2,128]{2,0,1:T(8,128)(2,1)}, bf16[256,2,128]{2,0,1:T(8,128)(2,1)S(1)}, u32[]{:S(2)}, u32[]{:S(2)}) collective-permute-start(bf16[256,2,128]{2,0,1:T(8,128)(2,1)} %get-tuple-element.308), channel_id=1, source_target_pairs={{0,4},{4,8},{8,12},{12,16},{16,20},{20,24},{24,28},{1,5},{5,9},{9,... | collective-permute-start | bytes 393224 | tf_op jit(solution)/shard_map/while/body/eval_jaxpr/ppermute | solution.py:16
  92.9 4.6 %collective-permute-start.1 = (bf16[256,2,128]{2,0,1:T(8,128)(2,1)S(1)}, bf16[256,2,128]{2,0,1:T(8,128)(2,1)S(1)}, u32[]{:S(2)}, u32[]{:S(2)}) collective-permute-start(bf16[256,2,128]{2,0,1:T(8,128)(2,1)S(1)} %get-tuple-element.309), channel_id=1, source_target_pairs={{0,4},{4,8},{8,12},{12,16},{16,20},{20,24},{24,28},{1,5},{5,9},{9,... | collective-permute-start | bytes 393224 | tf_op jit(solution)/shard_map/while/body/eval_jaxpr/ppermute | solution.py:16
  97.7 1.4 %fusion.40 = (f32[2,2,256]{2,1,0:T(2,128)S(1)}, bf16[2,2,256,256]{2,3,1,0:T(8,128)(2,1)S(1)}) fusion(bf16[256,2,2,128]{3,0,2,1:T(8,128)(2,1)} %get-tuple-element.323, bf16[256,2,128]{2,0,1:T(8,128)(2,1)S(1)} %collective-permute-done, pred[256,256]{0,1:T(8,128)(4,1)S(1)} %fusion.39), kind=kOutput, calls=%fused_computation.49.clone.1 | convolution fusion | flops 68418560 | bytes 987136 | tf_op jit(solution)/shard_map/while/body/eval_jaxpr/sgrh,kgh->grsk/dot_general | solution.py:41
  99.1 0.6 copy.45
  99.8 0.2 collective-permute-done.1
  100.0 0.4 convolution_add_fusion.2
  100.4 0.8 copy-done.2
  101.2 2.0 %divide_convert_fusion = bf16[2,2,256,128]{3,2,1,0:T(8,128)(2,1)} fusion(f32[2,2,256,128]{3,2,1,0:T(8,128)} %get-tuple-element.189, f32[2,2,256]{2,1,0:T(2,128)S(1)} %get-tuple-element.190), kind=kLoop, calls=%fused_computation.26 | loop fusion | flops 262144 | bytes 790528 | tf_op jit(solution)/shard_map/convert_element_type | solution.py:97
  103.3 0.7 convert_element_type.50
  103.9 15.4 %all-gather.2.cloned.1.call-done = bf16[256,16,128]{2,0,1:T(8,128)(2,1)} async-done(((bf16[256,4,128]{2,0,1:T(8,128)(2,1)}), bf16[256,16,128]{2,0,1:T(8,128)(2,1)}) %all-gather.2.cloned.1.call-update) | async-done | bytes 1048592 | tf_op jit(solution)/shard_map/all_gather | solution.py:100
  119.3 3.1 %multiply_reduce_fusion = (f32[256]{0:T(256)S(1)}, f32[256,768]{1,0:T(8,128)}) fusion(bf16[256,16,128]{2,0,1:T(8,128)(2,1)} %all-gather.2.cloned.1.call-done, bf16[16,128,768]{2,1,0:T(8,128)(2,1)S(1)} %copy-done), kind=kOutput, calls=%fused_computation.25 | convolution fusion | flops 805699328 | bytes 4981760 | tf_op jit(solution)/shard_map/dot_general | solution.py:103
  122.4 5.9 %psum.7 = f32[256]{0:T(256)S(1)} all-reduce(f32[256]{0:T(256)S(1)} %get-tuple-element.233), channel_id=1, replica_groups=mesh['ctx'=8,'tp'=4] {'tp'}, use_global_device_ids=true, to_apply=%region_5.6 | all-reduce | flops 256 | bytes 2048 | tf_op jit(solution)/shard_map/psum | solution.py:106
  128.3 2.1 %add_convert_fusion = bf16[256,768]{1,0:T(8,128)(2,1)} fusion(f32[256,768]{1,0:T(8,128)} %get-tuple-element.234, bf16[256,768]{1,0:T(8,128)(2,1)S(1)} %copy-done.4, f32[768]{0:T(1024)S(1)} %convert_element_type.50, f32[256]{0:T(256)S(1)} %add_rsqrt_fusion), kind=kLoop, calls=%fused_computation.24 | loop fusion | flops 983040 | bytes 1576960 | tf_op jit(solution)/shard_map/convert_element_type | solution.py:109
  (93 shorter events, 2.1 us)
Async XLA Ops:
  6.5 112.8 %copy-start = (bf16[16,128,768]{2,1,0:T(8,128)(2,1)S(1)}, bf16[16,128,768]{2,1,0:T(8,128)(2,1)}, u32[]{:S(2)}) copy-start(bf16[16,128,768]{2,1,0:T(8,128)(2,1)} %param.12) | copy-start | bytes 9437188
  6.5 4.8 %copy-start.3 = (bf16[256,2,128]{2,1,0:T(2,128)(2,1)S(1)}, bf16[256,2,128]{2,1,0:T(2,128)(2,1)}, u32[]{:S(2)}) copy-start(bf16[256,2,128]{2,1,0:T(2,128)(2,1)} %param.10) | copy-start | bytes 393220
  6.5 112.8 %all-gather.2.cloned.1.call-start = ((), (), s32[]{:S(2)}) async-start(), calls=%async_computation | async-start | bytes 1310720 | tf_op jit(solution)/shard_map/all_gather | solution.py:100
  13.1 3.0 %copy-start.6 = (bf16[256,2,128]{2,0,1:T(8,128)(2,1)}, bf16[256,2,128]{2,0,1:T(8,128)(2,1)S(1)}, u32[]{:S(2)}) copy-start(bf16[256,2,128]{2,0,1:T(8,128)(2,1)S(1)} %pad_maximum_fusion.1) | copy-start | bytes 393220
  14.3 1.8 %copy-start.5 = (bf16[256,2,2,128]{3,0,2,1:T(8,128)(2,1)}, bf16[256,2,2,128]{3,0,2,1:T(8,128)(2,1)S(1)}, u32[]{:S(2)}) copy-start(bf16[256,2,2,128]{3,0,2,1:T(8,128)(2,1)S(1)} %pad_maximum_fusion) | copy-start | bytes 786436
  14.3 1.8 %copy-start.7 = (bf16[256,2,128]{2,0,1:T(8,128)(2,1)S(1)}, bf16[256,2,128]{2,0,1:T(8,128)(2,1)}, u32[]{:S(2)}) copy-start(bf16[256,2,128]{2,0,1:T(8,128)(2,1)} %copy.20) | copy-start | bytes 393220
  16.1 8.5 %collective-permute-start = (bf16[256,2,128]{2,0,1:T(8,128)(2,1)}, bf16[256,2,128]{2,0,1:T(8,128)(2,1)S(1)}, u32[]{:S(2)}, u32[]{:S(2)}) collective-permute-start(bf16[256,2,128]{2,0,1:T(8,128)(2,1)} %get-tuple-element.308), channel_id=1, source_target_pairs={{0,4},{4,8},{8,12},{12,16},{16,20},{20,24},{24,28},{1,5},{5,9},{9,... | collective-permute-start | bytes 393224 | tf_op jit(solution)/shard_map/while/body/eval_jaxpr/ppermute | solution.py:16
  21.0 5.9 %collective-permute-start.1 = (bf16[256,2,128]{2,0,1:T(8,128)(2,1)S(1)}, bf16[256,2,128]{2,0,1:T(8,128)(2,1)S(1)}, u32[]{:S(2)}, u32[]{:S(2)}) collective-permute-start(bf16[256,2,128]{2,0,1:T(8,128)(2,1)S(1)} %get-tuple-element.309), channel_id=1, source_target_pairs={{0,4},{4,8},{8,12},{12,16},{16,20},{20,24},{24,28},{1,5},{5,9},{9,... | collective-permute-start | bytes 393224 | tf_op jit(solution)/shard_map/while/body/eval_jaxpr/ppermute | solution.py:16
  24.5 2.5 %copy-start.1 = (f32[2,2,256,128]{3,2,1,0:T(8,128)S(1)}, f32[2,2,256,128]{3,2,1,0:T(8,128)}, u32[]{:S(2)}) copy-start(f32[2,2,256,128]{3,2,1,0:T(8,128)} %get-tuple-element.306) | copy-start | bytes 1572868 | tf_op jit(solution)/shard_map/while
  27.4 0.8 copy-start.2
  28.2 8.9 %collective-permute-start = (bf16[256,2,128]{2,0,1:T(8,128)(2,1)}, bf16[256,2,128]{2,0,1:T(8,128)(2,1)S(1)}, u32[]{:S(2)}, u32[]{:S(2)}) collective-permute-start(bf16[256,2,128]{2,0,1:T(8,128)(2,1)} %get-tuple-element.308), channel_id=1, source_target_pairs={{0,4},{4,8},{8,12},{12,16},{16,20},{20,24},{24,28},{1,5},{5,9},{9,... | collective-permute-start | bytes 393224 | tf_op jit(solution)/shard_map/while/body/eval_jaxpr/ppermute | solution.py:16
  32.5 6.8 %collective-permute-start.1 = (bf16[256,2,128]{2,0,1:T(8,128)(2,1)S(1)}, bf16[256,2,128]{2,0,1:T(8,128)(2,1)S(1)}, u32[]{:S(2)}, u32[]{:S(2)}) collective-permute-start(bf16[256,2,128]{2,0,1:T(8,128)(2,1)S(1)} %get-tuple-element.309), channel_id=1, source_target_pairs={{0,4},{4,8},{8,12},{12,16},{16,20},{20,24},{24,28},{1,5},{5,9},{9,... | collective-permute-start | bytes 393224 | tf_op jit(solution)/shard_map/while/body/eval_jaxpr/ppermute | solution.py:16
  36.9 2.5 %copy-start.1 = (f32[2,2,256,128]{3,2,1,0:T(8,128)S(1)}, f32[2,2,256,128]{3,2,1,0:T(8,128)}, u32[]{:S(2)}) copy-start(f32[2,2,256,128]{3,2,1,0:T(8,128)} %get-tuple-element.306) | copy-start | bytes 1572868 | tf_op jit(solution)/shard_map/while
  39.8 0.8 copy-start.2
  40.6 8.7 %collective-permute-start = (bf16[256,2,128]{2,0,1:T(8,128)(2,1)}, bf16[256,2,128]{2,0,1:T(8,128)(2,1)S(1)}, u32[]{:S(2)}, u32[]{:S(2)}) collective-permute-start(bf16[256,2,128]{2,0,1:T(8,128)(2,1)} %get-tuple-element.308), channel_id=1, source_target_pairs={{0,4},{4,8},{8,12},{12,16},{16,20},{20,24},{24,28},{1,5},{5,9},{9,... | collective-permute-start | bytes 393224 | tf_op jit(solution)/shard_map/while/body/eval_jaxpr/ppermute | solution.py:16
  45.0 6.6 %collective-permute-start.1 = (bf16[256,2,128]{2,0,1:T(8,128)(2,1)S(1)}, bf16[256,2,128]{2,0,1:T(8,128)(2,1)S(1)}, u32[]{:S(2)}, u32[]{:S(2)}) collective-permute-start(bf16[256,2,128]{2,0,1:T(8,128)(2,1)S(1)} %get-tuple-element.309), channel_id=1, source_target_pairs={{0,4},{4,8},{8,12},{12,16},{16,20},{20,24},{24,28},{1,5},{5,9},{9,... | collective-permute-start | bytes 393224 | tf_op jit(solution)/shard_map/while/body/eval_jaxpr/ppermute | solution.py:16
  49.1 2.5 %copy-start.1 = (f32[2,2,256,128]{3,2,1,0:T(8,128)S(1)}, f32[2,2,256,128]{3,2,1,0:T(8,128)}, u32[]{:S(2)}) copy-start(f32[2,2,256,128]{3,2,1,0:T(8,128)} %get-tuple-element.306) | copy-start | bytes 1572868 | tf_op jit(solution)/shard_map/while
  52.0 0.8 copy-start.2
  52.8 8.2 %collective-permute-start = (bf16[256,2,128]{2,0,1:T(8,128)(2,1)}, bf16[256,2,128]{2,0,1:T(8,128)(2,1)S(1)}, u32[]{:S(2)}, u32[]{:S(2)}) collective-permute-start(bf16[256,2,128]{2,0,1:T(8,128)(2,1)} %get-tuple-element.308), channel_id=1, source_target_pairs={{0,4},{4,8},{8,12},{12,16},{16,20},{20,24},{24,28},{1,5},{5,9},{9,... | collective-permute-start | bytes 393224 | tf_op jit(solution)/shard_map/while/body/eval_jaxpr/ppermute | solution.py:16
  57.2 6.2 %collective-permute-start.1 = (bf16[256,2,128]{2,0,1:T(8,128)(2,1)S(1)}, bf16[256,2,128]{2,0,1:T(8,128)(2,1)S(1)}, u32[]{:S(2)}, u32[]{:S(2)}) collective-permute-start(bf16[256,2,128]{2,0,1:T(8,128)(2,1)S(1)} %get-tuple-element.309), channel_id=1, source_target_pairs={{0,4},{4,8},{8,12},{12,16},{16,20},{20,24},{24,28},{1,5},{5,9},{9,... | collective-permute-start | bytes 393224 | tf_op jit(solution)/shard_map/while/body/eval_jaxpr/ppermute | solution.py:16
  60.9 2.5 %copy-start.1 = (f32[2,2,256,128]{3,2,1,0:T(8,128)S(1)}, f32[2,2,256,128]{3,2,1,0:T(8,128)}, u32[]{:S(2)}) copy-start(f32[2,2,256,128]{3,2,1,0:T(8,128)} %get-tuple-element.306) | copy-start | bytes 1572868 | tf_op jit(solution)/shard_map/while
  63.8 0.8 copy-start.2
  64.6 8.6 %collective-permute-start = (bf16[256,2,128]{2,0,1:T(8,128)(2,1)}, bf16[256,2,128]{2,0,1:T(8,128)(2,1)S(1)}, u32[]{:S(2)}, u32[]{:S(2)}) collective-permute-start(bf16[256,2,128]{2,0,1:T(8,128)(2,1)} %get-tuple-element.308), channel_id=1, source_target_pairs={{0,4},{4,8},{8,12},{12,16},{16,20},{20,24},{24,28},{1,5},{5,9},{9,... | collective-permute-start | bytes 393224 | tf_op jit(solution)/shard_map/while/body/eval_jaxpr/ppermute | solution.py:16
  69.0 6.6 %collective-permute-start.1 = (bf16[256,2,128]{2,0,1:T(8,128)(2,1)S(1)}, bf16[256,2,128]{2,0,1:T(8,128)(2,1)S(1)}, u32[]{:S(2)}, u32[]{:S(2)}) collective-permute-start(bf16[256,2,128]{2,0,1:T(8,128)(2,1)S(1)} %get-tuple-element.309), channel_id=1, source_target_pairs={{0,4},{4,8},{8,12},{12,16},{16,20},{20,24},{24,28},{1,5},{5,9},{9,... | collective-permute-start | bytes 393224 | tf_op jit(solution)/shard_map/while/body/eval_jaxpr/ppermute | solution.py:16
  73.1 2.5 %copy-start.1 = (f32[2,2,256,128]{3,2,1,0:T(8,128)S(1)}, f32[2,2,256,128]{3,2,1,0:T(8,128)}, u32[]{:S(2)}) copy-start(f32[2,2,256,128]{3,2,1,0:T(8,128)} %get-tuple-element.306) | copy-start | bytes 1572868 | tf_op jit(solution)/shard_map/while
  76.0 0.8 copy-start.2
  76.8 8.2 %collective-permute-start = (bf16[256,2,128]{2,0,1:T(8,128)(2,1)}, bf16[256,2,128]{2,0,1:T(8,128)(2,1)S(1)}, u32[]{:S(2)}, u32[]{:S(2)}) collective-permute-start(bf16[256,2,128]{2,0,1:T(8,128)(2,1)} %get-tuple-element.308), channel_id=1, source_target_pairs={{0,4},{4,8},{8,12},{12,16},{16,20},{20,24},{24,28},{1,5},{5,9},{9,... | collective-permute-start | bytes 393224 | tf_op jit(solution)/shard_map/while/body/eval_jaxpr/ppermute | solution.py:16
  81.1 6.2 %collective-permute-start.1 = (bf16[256,2,128]{2,0,1:T(8,128)(2,1)S(1)}, bf16[256,2,128]{2,0,1:T(8,128)(2,1)S(1)}, u32[]{:S(2)}, u32[]{:S(2)}) collective-permute-start(bf16[256,2,128]{2,0,1:T(8,128)(2,1)S(1)} %get-tuple-element.309), channel_id=1, source_target_pairs={{0,4},{4,8},{8,12},{12,16},{16,20},{20,24},{24,28},{1,5},{5,9},{9,... | collective-permute-start | bytes 393224 | tf_op jit(solution)/shard_map/while/body/eval_jaxpr/ppermute | solution.py:16
  84.9 2.5 %copy-start.1 = (f32[2,2,256,128]{3,2,1,0:T(8,128)S(1)}, f32[2,2,256,128]{3,2,1,0:T(8,128)}, u32[]{:S(2)}) copy-start(f32[2,2,256,128]{3,2,1,0:T(8,128)} %get-tuple-element.306) | copy-start | bytes 1572868 | tf_op jit(solution)/shard_map/while
  87.8 0.8 copy-start.2
  88.6 9.1 %collective-permute-start = (bf16[256,2,128]{2,0,1:T(8,128)(2,1)}, bf16[256,2,128]{2,0,1:T(8,128)(2,1)S(1)}, u32[]{:S(2)}, u32[]{:S(2)}) collective-permute-start(bf16[256,2,128]{2,0,1:T(8,128)(2,1)} %get-tuple-element.308), channel_id=1, source_target_pairs={{0,4},{4,8},{8,12},{12,16},{16,20},{20,24},{24,28},{1,5},{5,9},{9,... | collective-permute-start | bytes 393224 | tf_op jit(solution)/shard_map/while/body/eval_jaxpr/ppermute | solution.py:16
  92.9 7.1 %collective-permute-start.1 = (bf16[256,2,128]{2,0,1:T(8,128)(2,1)S(1)}, bf16[256,2,128]{2,0,1:T(8,128)(2,1)S(1)}, u32[]{:S(2)}, u32[]{:S(2)}) collective-permute-start(bf16[256,2,128]{2,0,1:T(8,128)(2,1)S(1)} %get-tuple-element.309), channel_id=1, source_target_pairs={{0,4},{4,8},{8,12},{12,16},{16,20},{20,24},{24,28},{1,5},{5,9},{9,... | collective-permute-start | bytes 393224 | tf_op jit(solution)/shard_map/while/body/eval_jaxpr/ppermute | solution.py:16
  97.5 2.5 %copy-start.1 = (f32[2,2,256,128]{3,2,1,0:T(8,128)S(1)}, f32[2,2,256,128]{3,2,1,0:T(8,128)}, u32[]{:S(2)}) copy-start(f32[2,2,256,128]{3,2,1,0:T(8,128)} %get-tuple-element.306) | copy-start | bytes 1572868 | tf_op jit(solution)/shard_map/while
  100.4 0.8 copy-start.2
  101.2 27.1 %copy-start.4 = (bf16[256,768]{1,0:T(8,128)(2,1)S(1)}, bf16[256,768]{1,0:T(8,128)(2,1)}, u32[]{:S(2)}) copy-start(bf16[256,768]{1,0:T(8,128)(2,1)} %param.11) | copy-start | bytes 1179652
Sparse Core Ops, SparseCore 0:
  103.4 15.8 all-gather.1
where the time goes:
time: 138 us; the launch traced here: 137 us
  starting transfers between devices  58.8 us (43%)
  matrix products  17.8 us (13%)
  waiting for transfers between devices  16.7 us (12%)
  between operations  13.5 us (10%)
  other arithmetic  12.3 us (9%)
  local copies, waits for them, and re-layouts  11.6 us (8%)
  blocking collectives  5.85 us (4%)
    ppermute x14, starting transfers between devices, passed_along(): lax.ppermute(value, axis, [(source, source + steps) for source in range(f...  58.8 us
    all_gather x1, waiting for transfers between devices, local(): piece = lax.all_gather(attended, 'tp', axis=1, tiled=True)  15.4 us
    dot_general x8, matrix products, attend_block(): jnp.einsum('sgrh,kgh->grsk', rotary_queries, key_block, preferred_element...  10.6 us
    while x42, local copies, waits for them, and re-layouts  10.1 us
    psum x1, blocking collectives, local(): square_sums = lax.psum(jnp.sum(projected * projected, axis=1), 'tp')  5.85 us
    dot_general x8, matrix products, attend_block(): jnp.einsum('grsk,kgh->grsh', weights.astype(jnp.bfloat16), value_block, p...  4.09 us
    dot_general x1, matrix products, local(): jnp.dot(piece.reshape(rows, heads_in * head_size), weight_rows, preferred...  3.14 us
  transfers between devices with their start and end apart: 15, of which 8 were waited for; matrix products, arithmetic and copies ran while one was open for 12% of the time, Pallas kernels for 0%

commit v1 on v0

--- a/solution.py
+++ b/solution.py
@@ -97,7 +97,24 @@
     attended = (numerators / denominators[..., None]).astype(jnp.bfloat16)
     attended = jnp.transpose(attended, (2, 0, 1, 3)).reshape(rows, q_heads, head_size)
     local_cols = out_weight.shape[2]
-    piece = lax.all_gather(attended, "tp", axis=1, tiled=True)
+    size, index, rows_2 = (lax.axis_size("tp"), lax.axis_index("tp"), attended.shape[1])
+    right = [(i, (i + 1) % size) for i in range(size)]
+    left = [(i, (i - 1) % size) for i in range(size)]
+    out = jnp.zeros((*attended.shape[:1], size * rows_2, *attended.shape[1 + 1 :]), attended.dtype)
+    out = lax.dynamic_update_slice_in_dim(out, attended, index * rows_2, axis=1)
+    from_left = from_right = attended
+    half = size // 2
+    for turn in range(1, half + 1):
+        from_left = lax.ppermute(from_left, "tp", right)
+        out = lax.dynamic_update_slice_in_dim(
+            out, from_left, (index - turn) % size * rows_2, axis=1
+        )
+        if turn < size - half:
+            from_right = lax.ppermute(from_right, "tp", left)
+            out = lax.dynamic_update_slice_in_dim(
+                out, from_right, (index + turn) % size * rows_2, axis=1
+            )
+    piece = out
     heads_in = piece.shape[1]
     weight_rows = out_weight.reshape(heads_in * head_size, local_cols)
     projected = jnp.dot(

time: 138 us -> 129 us (0.935)
  between operations: 13.5 us -> 0.11 us
  local copies, waits for them, and re-layouts: 11.6 us -> 18.7 us
  waiting for transfers between devices: 16.7 us -> 13 us
  blocking collectives: 5.85 us -> 8.17 us
  other arithmetic: 12.3 us -> 10.7 us
    all_gather x1 -> x0, waiting for transfers between devices: 15.4 us -> none  [local(): piece = lax.all_gather(attended, 'tp', axis=1, tiled=True)]
    ppermute x14, waiting for transfers between devices: 1.3 us -> 7.89 us  [passed_along(): lax.ppermute(value, axis, [(source, source + steps) for source in range(f...]
    dynamic_update_slice x0 -> x4, local copies, waits for them, and re-layouts: none -> 5.78 us  [the longest x2 3.39 us: local(): lax.dynamic_update_slice_in_dim(out, from_left, (index - turn) % size * r...]
    ppermute x0 -> x3, waiting for transfers between devices: none -> 5.14 us  [the longest x2 5.14 us: local(): from_left = lax.ppermute(from_left, 'tp', right)]
    psum x1, blocking collectives: 5.85 us -> 8.17 us  [local(): square_sums = lax.psum(jnp.sum(projected * projected, axis=1), 'tp')]
    ppermute x0 -> x3, starting transfers between devices: none -> 1.93 us  [the longest x1 1.73 us: local(): from_right = lax.ppermute(from_right, 'tp', left)]
    ppermute x14, starting transfers between devices: 58.8 us -> 57 us  [passed_along(): lax.ppermute(value, axis, [(source, source + steps) for source in range(f...]
  transfers between devices with their start and end apart: 15 -> 17, of which waited for: 8 -> 8; matrix products, arithmetic and copies ran while one was open for 12% -> 13% of each run, Pallas kernels for 0% -> 0%
where the time goes in v1:
time: 129 us; the launch traced here: 128 us
  starting transfers between devices  59 us (46%)
  local copies, waits for them, and re-layouts  18.7 us (14%)
  matrix products  17.8 us (14%)
  waiting for transfers between devices  13 us (10%)
  other arithmetic  10.7 us (8%)
  blocking collectives  8.17 us (6%)
    ppermute x14, starting transfers between devices, passed_along(): lax.ppermute(value, axis, [(source, source + steps) for source in range(f...  57 us
    dot_general x8, matrix products, attend_block(): jnp.einsum('sgrh,kgh->grsk', rotary_queries, key_block, preferred_element...  10.6 us
    while x42, local copies, waits for them, and re-layouts  10.2 us
    psum x1, blocking collectives, local(): square_sums = lax.psum(jnp.sum(projected * projected, axis=1), 'tp')  8.17 us
    ppermute x14, waiting for transfers between devices, passed_along(): lax.ppermute(value, axis, [(source, source + steps) for source in range(f...  7.89 us
    ppermute x2, waiting for transfers between devices, local(): from_left = lax.ppermute(from_left, 'tp', right)  5.14 us
    dot_general x8, matrix products, attend_block(): jnp.einsum('grsk,kgh->grsh', weights.astype(jnp.bfloat16), value_block, p...  4.09 us
    dynamic_update_slice x2, local copies, waits for them, and re-layouts, local(): lax.dynamic_update_slice_in_dim(out, from_left, (index - turn) % size * r...  3.39 us
  transfers between devices with their start and end apart: 17, of which 8 were waited for; matrix products, arithmetic and copies ran while one was open for 13% of the time, Pallas kernels for 0%

profile of v1, /device:TPU:0, one launch (start us, length us, event | category | flops | bytes accessed | tf_op | source)
XLA Modules:
  0.0 128.2 jit_solution(11443161821394218355)
XLA Ops:
  0.1 1.2 convert_element_type.47
  1.3 0.5 multiply_cosine_fusion
  1.8 0.5 subtract_convert_fusion
  2.4 0.7 copy.10
  3.2 0.8 subtract_convert_fusion.1
  4.0 0.7 copy.13
  4.7 1.1 pad_maximum_fusion
  5.8 1.2 pad_maximum_fusion.1
  7.6 1.2 fusion.15
  8.8 90.0 %while.21 = (s32[]{:T(128)}, f32[2,2,256,128]{3,2,1,0:T(8,128)}, f32[2,2,256]{2,1,0:T(2,128)S(1)}, bf16[256,2,128]{2,0,1:T(8,128)(2,1)S(1)}, bf16[256,2,128]{2,0...) while((s32[]{:T(128)}, f32[2,2,256,128]{3,2,1,0:T(8,128)}, ...), condition=%wide.region_3.4_spmd, body=%wide.region_1.3_spmd.sunk | while | flops 135988224 | bytes 8540965 | solution.py:93
  8.8 4.9 %collective-permute-start = (bf16[256,2,128]{2,0,1:T(8,128)(2,1)S(1)}, bf16[256,2,128]{2,0,1:T(8,128)(2,1)S(1)}, u32[]{:S(2)}, u32[]{:S(2)}) collective-permute-start(bf16[256,2,128]{2,0,1:T(8,128)(2,1)S(1)} %get-tuple-element.300), channel_id=1, source_target_pairs={{0,4},{4,8},{8,12},{12,16},{16,20},{20,24},{24,28},{1,5},{5,9},{9,... | collective-permute-start | bytes 393224 | tf_op jit(solution)/shard_map/while/body/eval_jaxpr/ppermute | solution.py:16
  13.6 3.4 %collective-permute-start.1 = (bf16[256,2,128]{2,0,1:T(8,128)(2,1)}, bf16[256,2,128]{2,0,1:T(8,128)(2,1)S(1)}, u32[]{:S(2)}, u32[]{:S(2)}) collective-permute-start(bf16[256,2,128]{2,0,1:T(8,128)(2,1)} %get-tuple-element.301), channel_id=1, source_target_pairs={{0,4},{4,8},{8,12},{12,16},{16,20},{20,24},{24,28},{1,5},{5,9},{9,... | collective-permute-start | bytes 393224 | tf_op jit(solution)/shard_map/while/body/eval_jaxpr/ppermute | solution.py:16
  17.3 1.4 %fusion.40 = (f32[2,2,256]{2,1,0:T(2,128)S(1)}, bf16[2,2,256,256]{2,3,1,0:T(8,128)(2,1)S(1)}) fusion(bf16[256,2,2,128]{3,0,2,1:T(8,128)(2,1)} %get-tuple-element.315, bf16[256,2,128]{2,0,1:T(8,128)(2,1)S(1)} %collective-permute-done, pred[256,256]{0,1:T(8,128)(4,1)S(1)} %fusion.39), kind=kOutput, calls=%fused_computation.53.clone.1 | convolution fusion | flops 68418560 | bytes 987136 | tf_op jit(solution)/shard_map/while/body/eval_jaxpr/sgrh,kgh->grsk/dot_general | solution.py:41
  18.8 1.1 collective-permute-done.1
  19.9 0.7 copy.39
  21.0 0.8 copy-done.2
  21.8 4.2 %collective-permute-start = (bf16[256,2,128]{2,0,1:T(8,128)(2,1)S(1)}, bf16[256,2,128]{2,0,1:T(8,128)(2,1)S(1)}, u32[]{:S(2)}, u32[]{:S(2)}) collective-permute-start(bf16[256,2,128]{2,0,1:T(8,128)(2,1)S(1)} %get-tuple-element.300), channel_id=1, source_target_pairs={{0,4},{4,8},{8,12},{12,16},{16,20},{20,24},{24,28},{1,5},{5,9},{9,... | collective-permute-start | bytes 393224 | tf_op jit(solution)/shard_map/while/body/eval_jaxpr/ppermute | solution.py:16
  26.0 4.3 %collective-permute-start.1 = (bf16[256,2,128]{2,0,1:T(8,128)(2,1)}, bf16[256,2,128]{2,0,1:T(8,128)(2,1)S(1)}, u32[]{:S(2)}, u32[]{:S(2)}) collective-permute-start(bf16[256,2,128]{2,0,1:T(8,128)(2,1)} %get-tuple-element.301), channel_id=1, source_target_pairs={{0,4},{4,8},{8,12},{12,16},{16,20},{20,24},{24,28},{1,5},{5,9},{9,... | collective-permute-start | bytes 393224 | tf_op jit(solution)/shard_map/while/body/eval_jaxpr/ppermute | solution.py:16
  30.6 1.4 %fusion.40 = (f32[2,2,256]{2,1,0:T(2,128)S(1)}, bf16[2,2,256,256]{2,3,1,0:T(8,128)(2,1)S(1)}) fusion(bf16[256,2,2,128]{3,0,2,1:T(8,128)(2,1)} %get-tuple-element.315, bf16[256,2,128]{2,0,1:T(8,128)(2,1)S(1)} %collective-permute-done, pred[256,256]{0,1:T(8,128)(4,1)S(1)} %fusion.39), kind=kOutput, calls=%fused_computation.53.clone.1 | convolution fusion | flops 68418560 | bytes 987136 | tf_op jit(solution)/shard_map/while/body/eval_jaxpr/sgrh,kgh->grsk/dot_general | solution.py:41
  32.0 1.1 collective-permute-done.1
  33.2 0.7 copy.39
  34.3 0.8 copy-done.2
  35.1 4.2 %collective-permute-start = (bf16[256,2,128]{2,0,1:T(8,128)(2,1)S(1)}, bf16[256,2,128]{2,0,1:T(8,128)(2,1)S(1)}, u32[]{:S(2)}, u32[]{:S(2)}) collective-permute-start(bf16[256,2,128]{2,0,1:T(8,128)(2,1)S(1)} %get-tuple-element.300), channel_id=1, source_target_pairs={{0,4},{4,8},{8,12},{12,16},{16,20},{20,24},{24,28},{1,5},{5,9},{9,... | collective-permute-start | bytes 393224 | tf_op jit(solution)/shard_map/while/body/eval_jaxpr/ppermute | solution.py:16
  39.3 3.5 %collective-permute-start.1 = (bf16[256,2,128]{2,0,1:T(8,128)(2,1)}, bf16[256,2,128]{2,0,1:T(8,128)(2,1)S(1)}, u32[]{:S(2)}, u32[]{:S(2)}) collective-permute-start(bf16[256,2,128]{2,0,1:T(8,128)(2,1)} %get-tuple-element.301), channel_id=1, source_target_pairs={{0,4},{4,8},{8,12},{12,16},{16,20},{20,24},{24,28},{1,5},{5,9},{9,... | collective-permute-start | bytes 393224 | tf_op jit(solution)/shard_map/while/body/eval_jaxpr/ppermute | solution.py:16
  43.0 1.4 %fusion.40 = (f32[2,2,256]{2,1,0:T(2,128)S(1)}, bf16[2,2,256,256]{2,3,1,0:T(8,128)(2,1)S(1)}) fusion(bf16[256,2,2,128]{3,0,2,1:T(8,128)(2,1)} %get-tuple-element.315, bf16[256,2,128]{2,0,1:T(8,128)(2,1)S(1)} %collective-permute-done, pred[256,256]{0,1:T(8,128)(4,1)S(1)} %fusion.39), kind=kOutput, calls=%fused_computation.53.clone.1 | convolution fusion | flops 68418560 | bytes 987136 | tf_op jit(solution)/shard_map/while/body/eval_jaxpr/sgrh,kgh->grsk/dot_general | solution.py:41
  44.5 1.1 collective-permute-done.1
  45.6 0.7 copy.39
  46.7 0.8 copy-done.2
  47.5 4.2 %collective-permute-start = (bf16[256,2,128]{2,0,1:T(8,128)(2,1)S(1)}, bf16[256,2,128]{2,0,1:T(8,128)(2,1)S(1)}, u32[]{:S(2)}, u32[]{:S(2)}) collective-permute-start(bf16[256,2,128]{2,0,1:T(8,128)(2,1)S(1)} %get-tuple-element.300), channel_id=1, source_target_pairs={{0,4},{4,8},{8,12},{12,16},{16,20},{20,24},{24,28},{1,5},{5,9},{9,... | collective-permute-start | bytes 393224 | tf_op jit(solution)/shard_map/while/body/eval_jaxpr/ppermute | solution.py:16
  51.7 4.3 %collective-permute-start.1 = (bf16[256,2,128]{2,0,1:T(8,128)(2,1)}, bf16[256,2,128]{2,0,1:T(8,128)(2,1)S(1)}, u32[]{:S(2)}, u32[]{:S(2)}) collective-permute-start(bf16[256,2,128]{2,0,1:T(8,128)(2,1)} %get-tuple-element.301), channel_id=1, source_target_pairs={{0,4},{4,8},{8,12},{12,16},{16,20},{20,24},{24,28},{1,5},{5,9},{9,... | collective-permute-start | bytes 393224 | tf_op jit(solution)/shard_map/while/body/eval_jaxpr/ppermute | solution.py:16
  56.2 1.4 %fusion.40 = (f32[2,2,256]{2,1,0:T(2,128)S(1)}, bf16[2,2,256,256]{2,3,1,0:T(8,128)(2,1)S(1)}) fusion(bf16[256,2,2,128]{3,0,2,1:T(8,128)(2,1)} %get-tuple-element.315, bf16[256,2,128]{2,0,1:T(8,128)(2,1)S(1)} %collective-permute-done, pred[256,256]{0,1:T(8,128)(4,1)S(1)} %fusion.39), kind=kOutput, calls=%fused_computation.53.clone.1 | convolution fusion | flops 68418560 | bytes 987136 | tf_op jit(solution)/shard_map/while/body/eval_jaxpr/sgrh,kgh->grsk/dot_general | solution.py:41
  57.7 1.1 collective-permute-done.1
  58.8 0.7 copy.39
  59.9 0.8 copy-done.2
  60.7 4.2 %collective-permute-start = (bf16[256,2,128]{2,0,1:T(8,128)(2,1)S(1)}, bf16[256,2,128]{2,0,1:T(8,128)(2,1)S(1)}, u32[]{:S(2)}, u32[]{:S(2)}) collective-permute-start(bf16[256,2,128]{2,0,1:T(8,128)(2,1)S(1)} %get-tuple-element.300), channel_id=1, source_target_pairs={{0,4},{4,8},{8,12},{12,16},{16,20},{20,24},{24,28},{1,5},{5,9},{9,... | collective-permute-start | bytes 393224 | tf_op jit(solution)/shard_map/while/body/eval_jaxpr/ppermute | solution.py:16
  65.0 3.5 %collective-permute-start.1 = (bf16[256,2,128]{2,0,1:T(8,128)(2,1)}, bf16[256,2,128]{2,0,1:T(8,128)(2,1)S(1)}, u32[]{:S(2)}, u32[]{:S(2)}) collective-permute-start(bf16[256,2,128]{2,0,1:T(8,128)(2,1)} %get-tuple-element.301), channel_id=1, source_target_pairs={{0,4},{4,8},{8,12},{12,16},{16,20},{20,24},{24,28},{1,5},{5,9},{9,... | collective-permute-start | bytes 393224 | tf_op jit(solution)/shard_map/while/body/eval_jaxpr/ppermute | solution.py:16
  68.6 1.4 %fusion.40 = (f32[2,2,256]{2,1,0:T(2,128)S(1)}, bf16[2,2,256,256]{2,3,1,0:T(8,128)(2,1)S(1)}) fusion(bf16[256,2,2,128]{3,0,2,1:T(8,128)(2,1)} %get-tuple-element.315, bf16[256,2,128]{2,0,1:T(8,128)(2,1)S(1)} %collective-permute-done, pred[256,256]{0,1:T(8,128)(4,1)S(1)} %fusion.39), kind=kOutput, calls=%fused_computation.53.clone.1 | convolution fusion | flops 68418560 | bytes 987136 | tf_op jit(solution)/shard_map/while/body/eval_jaxpr/sgrh,kgh->grsk/dot_general | solution.py:41
  70.1 1.1 collective-permute-done.1
  71.2 0.7 copy.39
  72.3 0.8 copy-done.2
  73.1 4.2 %collective-permute-start = (bf16[256,2,128]{2,0,1:T(8,128)(2,1)S(1)}, bf16[256,2,128]{2,0,1:T(8,128)(2,1)S(1)}, u32[]{:S(2)}, u32[]{:S(2)}) collective-permute-start(bf16[256,2,128]{2,0,1:T(8,128)(2,1)S(1)} %get-tuple-element.300), channel_id=1, source_target_pairs={{0,4},{4,8},{8,12},{12,16},{16,20},{20,24},{24,28},{1,5},{5,9},{9,... | collective-permute-start | bytes 393224 | tf_op jit(solution)/shard_map/while/body/eval_jaxpr/ppermute | solution.py:16
  77.4 4.3 %collective-permute-start.1 = (bf16[256,2,128]{2,0,1:T(8,128)(2,1)}, bf16[256,2,128]{2,0,1:T(8,128)(2,1)S(1)}, u32[]{:S(2)}, u32[]{:S(2)}) collective-permute-start(bf16[256,2,128]{2,0,1:T(8,128)(2,1)} %get-tuple-element.301), channel_id=1, source_target_pairs={{0,4},{4,8},{8,12},{12,16},{16,20},{20,24},{24,28},{1,5},{5,9},{9,... | collective-permute-start | bytes 393224 | tf_op jit(solution)/shard_map/while/body/eval_jaxpr/ppermute | solution.py:16
  81.9 1.4 %fusion.40 = (f32[2,2,256]{2,1,0:T(2,128)S(1)}, bf16[2,2,256,256]{2,3,1,0:T(8,128)(2,1)S(1)}) fusion(bf16[256,2,2,128]{3,0,2,1:T(8,128)(2,1)} %get-tuple-element.315, bf16[256,2,128]{2,0,1:T(8,128)(2,1)S(1)} %collective-permute-done, pred[256,256]{0,1:T(8,128)(4,1)S(1)} %fusion.39), kind=kOutput, calls=%fused_computation.53.clone.1 | convolution fusion | flops 68418560 | bytes 987136 | tf_op jit(solution)/shard_map/while/body/eval_jaxpr/sgrh,kgh->grsk/dot_general | solution.py:41
  83.3 1.1 collective-permute-done.1
  84.5 0.7 copy.39
  85.6 0.8 copy-done.2
  86.4 4.2 %collective-permute-start = (bf16[256,2,128]{2,0,1:T(8,128)(2,1)S(1)}, bf16[256,2,128]{2,0,1:T(8,128)(2,1)S(1)}, u32[]{:S(2)}, u32[]{:S(2)}) collective-permute-start(bf16[256,2,128]{2,0,1:T(8,128)(2,1)S(1)} %get-tuple-element.300), channel_id=1, source_target_pairs={{0,4},{4,8},{8,12},{12,16},{16,20},{20,24},{24,28},{1,5},{5,9},{9,... | collective-permute-start | bytes 393224 | tf_op jit(solution)/shard_map/while/body/eval_jaxpr/ppermute | solution.py:16
  90.6 3.5 %collective-permute-start.1 = (bf16[256,2,128]{2,0,1:T(8,128)(2,1)}, bf16[256,2,128]{2,0,1:T(8,128)(2,1)S(1)}, u32[]{:S(2)}, u32[]{:S(2)}) collective-permute-start(bf16[256,2,128]{2,0,1:T(8,128)(2,1)} %get-tuple-element.301), channel_id=1, source_target_pairs={{0,4},{4,8},{8,12},{12,16},{16,20},{20,24},{24,28},{1,5},{5,9},{9,... | collective-permute-start | bytes 393224 | tf_op jit(solution)/shard_map/while/body/eval_jaxpr/ppermute | solution.py:16
  94.3 1.4 %fusion.40 = (f32[2,2,256]{2,1,0:T(2,128)S(1)}, bf16[2,2,256,256]{2,3,1,0:T(8,128)(2,1)S(1)}) fusion(bf16[256,2,2,128]{3,0,2,1:T(8,128)(2,1)} %get-tuple-element.315, bf16[256,2,128]{2,0,1:T(8,128)(2,1)S(1)} %collective-permute-done, pred[256,256]{0,1:T(8,128)(4,1)S(1)} %fusion.39), kind=kOutput, calls=%fused_computation.53.clone.1 | convolution fusion | flops 68418560 | bytes 987136 | tf_op jit(solution)/shard_map/while/body/eval_jaxpr/sgrh,kgh->grsk/dot_general | solution.py:41
  95.8 1.1 collective-permute-done.1
  96.9 0.7 copy.39
  98.0 0.8 copy-done.2
  98.8 1.2 divide_convert_fusion
  100.1 1.7 %collective-permute-start.3 = (bf16[256,4,128]{2,0,1:T(8,128)(2,1)S(1)}, bf16[256,4,128]{2,0,1:T(8,128)(2,1)}, u32[]{:S(2)}, u32[]{:S(2)}) collective-permute-start(bf16[256,4,128]{2,0,1:T(8,128)(2,1)S(1)} %bitcast.50), channel_id=1, source_target_pairs={{0,3},{1,0},{2,1},{3,2},{4,7},{5,4},{6,5},{7,6},{8,11},{9,8},{10,9... | collective-permute-start | bytes 786440 | tf_op jit(solution)/shard_map/ppermute | solution.py:113
  101.9 5.1 %collective-permute-done.2 = bf16[256,4,128]{2,0,1:T(8,128)(2,1)} collective-permute-done((bf16[256,4,128]{2,0,1:T(8,128)(2,1)S(1)}, bf16[256,4,128]{2,0,1:T(8,128)(2,1)}, u32[]{:S(2)}, u32[]{:S(2)}) %collective-permute-start.2) | collective-permute-done | bytes 262176 | tf_op jit(solution)/shard_map/ppermute | solution.py:108
  107.1 1.2 broadcast_in_dim.66
  108.3 0.7 constant_dynamic-update-slice_fusion.3
  109.0 0.7 convert_element_type.50
  109.7 1.7 %constant_dynamic-update-slice_fusion.2 = bf16[256,16,128]{2,0,1:T(8,128)(2,1)} fusion(bf16[256,16,128]{2,0,1:T(8,128)(2,1)} %constant_dynamic-update-slice_fusion.3, bf16[256,4,128]{2,0,1:T(8,128)(2,1)} %collective-permute-done.2, s32[]{:T(128)S(6)} %select_n.44), kind=kLoop, calls=%fused_computation.48 | loop fusion | bytes 524292 | tf_op jit(solution)/shard_map/dynamic_update_slice | solution.py:109
  111.3 1.7 %constant_dynamic-update-slice_fusion.1 = bf16[256,16,128]{2,0,1:T(8,128)(2,1)} fusion(bf16[256,16,128]{2,0,1:T(8,128)(2,1)} %constant_dynamic-update-slice_fusion.2, bf16[256,4,128]{2,0,1:T(8,128)(2,1)} %collective-permute-done.3, s32[]{:T(128)S(6)} %select_n.46), kind=kLoop, calls=%fused_computation.47 | loop fusion | bytes 524292 | tf_op jit(solution)/shard_map/dynamic_update_slice | solution.py:114
  113.1 1.7 %constant_dynamic-update-slice_fusion = bf16[256,16,128]{2,0,1:T(8,128)(2,1)} fusion(bf16[256,16,128]{2,0,1:T(8,128)(2,1)} %constant_dynamic-update-slice_fusion.1, bf16[256,4,128]{2,0,1:T(8,128)(2,1)} %collective-permute-done.4, s32[]{:T(128)S(6)} %select_n.48), kind=kLoop, calls=%fused_computation.46 | loop fusion | bytes 524292 | tf_op jit(solution)/shard_map/dynamic_update_slice | solution.py:109
  114.8 3.1 %multiply_reduce_fusion = (f32[256]{0:T(256)S(1)}, f32[256,768]{1,0:T(8,128)}) fusion(bf16[256,16,128]{2,0,1:T(8,128)(2,1)} %constant_dynamic-update-slice_fusion, bf16[16,128,768]{2,1,0:T(8,128)(2,1)S(1)} %copy-done), kind=kOutput, calls=%fused_computation.25 | convolution fusion | flops 805699328 | bytes 4981760 | tf_op jit(solution)/shard_map/dot_general | solution.py:120
  117.9 8.2 %psum.7 = f32[256]{0:T(256)S(1)} all-reduce(f32[256]{0:T(256)S(1)} %get-tuple-element.225), channel_id=1, replica_groups=mesh['ctx'=8,'tp'=4] {'tp'}, use_global_device_ids=true, to_apply=%region_5.6 | all-reduce | flops 256 | bytes 2048 | tf_op jit(solution)/shard_map/psum | solution.py:123
  126.1 2.1 %add_convert_fusion = bf16[256,768]{1,0:T(8,128)(2,1)} fusion(f32[256,768]{1,0:T(8,128)} %get-tuple-element.226, bf16[256,768]{1,0:T(8,128)(2,1)S(1)} %copy-done.4, f32[768]{0:T(1024)S(1)} %convert_element_type.50, f32[256]{0:T(256)S(1)} %add_rsqrt_fusion), kind=kLoop, calls=%fused_computation.24 | loop fusion | flops 983040 | bytes 1576960 | tf_op jit(solution)/shard_map/convert_element_type | solution.py:126
  (99 shorter events, 5.2 us)
Async XLA Ops:
  0.0 114.8 %copy-start = (bf16[16,128,768]{2,1,0:T(8,128)(2,1)S(1)}, bf16[16,128,768]{2,1,0:T(8,128)(2,1)}, u32[]{:S(2)}) copy-start(bf16[16,128,768]{2,1,0:T(8,128)(2,1)} %param.12) | copy-start | bytes 9437188
  0.0 4.0 %copy-start.3 = (bf16[256,2,128]{2,1,0:T(2,128)(2,1)S(1)}, bf16[256,2,128]{2,1,0:T(2,128)(2,1)}, u32[]{:S(2)}) copy-start(bf16[256,2,128]{2,1,0:T(2,128)(2,1)} %param.10) | copy-start | bytes 393220
  0.0 3.1 %copy-start.6 = (bf16[256,2,128]{2,1,0:T(2,128)(2,1)S(1)}, bf16[256,2,128]{2,1,0:T(2,128)(2,1)}, u32[]{:S(2)}) copy-start(bf16[256,2,128]{2,1,0:T(2,128)(2,1)} %param.9) | copy-start | bytes 393220
  5.8 3.0 %copy-start.5 = (bf16[256,2,2,128]{3,0,2,1:T(8,128)(2,1)}, bf16[256,2,2,128]{3,0,2,1:T(8,128)(2,1)S(1)}, u32[]{:S(2)}) copy-start(bf16[256,2,2,128]{3,0,2,1:T(8,128)(2,1)S(1)} %pad_maximum_fusion) | copy-start | bytes 786436
  8.8 8.5 %collective-permute-start = (bf16[256,2,128]{2,0,1:T(8,128)(2,1)S(1)}, bf16[256,2,128]{2,0,1:T(8,128)(2,1)S(1)}, u32[]{:S(2)}, u32[]{:S(2)}) collective-permute-start(bf16[256,2,128]{2,0,1:T(8,128)(2,1)S(1)} %get-tuple-element.300), channel_id=1, source_target_pairs={{0,4},{4,8},{8,12},{12,16},{16,20},{20,24},{24,28},{1,5},{5,9},{9,... | collective-permute-start | bytes 393224 | tf_op jit(solution)/shard_map/while/body/eval_jaxpr/ppermute | solution.py:16
  13.6 6.2 %collective-permute-start.1 = (bf16[256,2,128]{2,0,1:T(8,128)(2,1)}, bf16[256,2,128]{2,0,1:T(8,128)(2,1)S(1)}, u32[]{:S(2)}, u32[]{:S(2)}) collective-permute-start(bf16[256,2,128]{2,0,1:T(8,128)(2,1)} %get-tuple-element.301), channel_id=1, source_target_pairs={{0,4},{4,8},{8,12},{12,16},{16,20},{20,24},{24,28},{1,5},{5,9},{9,... | collective-permute-start | bytes 393224 | tf_op jit(solution)/shard_map/while/body/eval_jaxpr/ppermute | solution.py:16
  17.1 3.4 %copy-start.1 = (f32[2,2,256,128]{3,2,1,0:T(8,128)S(1)}, f32[2,2,256,128]{3,2,1,0:T(8,128)}, u32[]{:S(2)}) copy-start(f32[2,2,256,128]{3,2,1,0:T(8,128)} %get-tuple-element.298) | copy-start | bytes 1572868 | tf_op jit(solution)/shard_map/while
  21.0 0.8 copy-start.2
  21.8 8.8 %collective-permute-start = (bf16[256,2,128]{2,0,1:T(8,128)(2,1)S(1)}, bf16[256,2,128]{2,0,1:T(8,128)(2,1)S(1)}, u32[]{:S(2)}, u32[]{:S(2)}) collective-permute-start(bf16[256,2,128]{2,0,1:T(8,128)(2,1)S(1)} %get-tuple-element.300), channel_id=1, source_target_pairs={{0,4},{4,8},{8,12},{12,16},{16,20},{20,24},{24,28},{1,5},{5,9},{9,... | collective-permute-start | bytes 393224 | tf_op jit(solution)/shard_map/while/body/eval_jaxpr/ppermute | solution.py:16
  26.0 7.2 %collective-permute-start.1 = (bf16[256,2,128]{2,0,1:T(8,128)(2,1)}, bf16[256,2,128]{2,0,1:T(8,128)(2,1)S(1)}, u32[]{:S(2)}, u32[]{:S(2)}) collective-permute-start(bf16[256,2,128]{2,0,1:T(8,128)(2,1)} %get-tuple-element.301), channel_id=1, source_target_pairs={{0,4},{4,8},{8,12},{12,16},{16,20},{20,24},{24,28},{1,5},{5,9},{9,... | collective-permute-start | bytes 393224 | tf_op jit(solution)/shard_map/while/body/eval_jaxpr/ppermute | solution.py:16
  30.4 3.4 %copy-start.1 = (f32[2,2,256,128]{3,2,1,0:T(8,128)S(1)}, f32[2,2,256,128]{3,2,1,0:T(8,128)}, u32[]{:S(2)}) copy-start(f32[2,2,256,128]{3,2,1,0:T(8,128)} %get-tuple-element.298) | copy-start | bytes 1572868 | tf_op jit(solution)/shard_map/while
  34.2 0.8 copy-start.2
  35.1 7.9 %collective-permute-start = (bf16[256,2,128]{2,0,1:T(8,128)(2,1)S(1)}, bf16[256,2,128]{2,0,1:T(8,128)(2,1)S(1)}, u32[]{:S(2)}, u32[]{:S(2)}) collective-permute-start(bf16[256,2,128]{2,0,1:T(8,128)(2,1)S(1)} %get-tuple-element.300), channel_id=1, source_target_pairs={{0,4},{4,8},{8,12},{12,16},{16,20},{20,24},{24,28},{1,5},{5,9},{9,... | collective-permute-start | bytes 393224 | tf_op jit(solution)/shard_map/while/body/eval_jaxpr/ppermute | solution.py:16
  39.3 6.3 %collective-permute-start.1 = (bf16[256,2,128]{2,0,1:T(8,128)(2,1)}, bf16[256,2,128]{2,0,1:T(8,128)(2,1)S(1)}, u32[]{:S(2)}, u32[]{:S(2)}) collective-permute-start(bf16[256,2,128]{2,0,1:T(8,128)(2,1)} %get-tuple-element.301), channel_id=1, source_target_pairs={{0,4},{4,8},{8,12},{12,16},{16,20},{20,24},{24,28},{1,5},{5,9},{9,... | collective-permute-start | bytes 393224 | tf_op jit(solution)/shard_map/while/body/eval_jaxpr/ppermute | solution.py:16
  42.8 3.4 %copy-start.1 = (f32[2,2,256,128]{3,2,1,0:T(8,128)S(1)}, f32[2,2,256,128]{3,2,1,0:T(8,128)}, u32[]{:S(2)}) copy-start(f32[2,2,256,128]{3,2,1,0:T(8,128)} %get-tuple-element.298) | copy-start | bytes 1572868 | tf_op jit(solution)/shard_map/while
  46.7 0.8 copy-start.2
  47.5 8.7 %collective-permute-start = (bf16[256,2,128]{2,0,1:T(8,128)(2,1)S(1)}, bf16[256,2,128]{2,0,1:T(8,128)(2,1)S(1)}, u32[]{:S(2)}, u32[]{:S(2)}) collective-permute-start(bf16[256,2,128]{2,0,1:T(8,128)(2,1)S(1)} %get-tuple-element.300), channel_id=1, source_target_pairs={{0,4},{4,8},{8,12},{12,16},{16,20},{20,24},{24,28},{1,5},{5,9},{9,... | collective-permute-start | bytes 393224 | tf_op jit(solution)/shard_map/while/body/eval_jaxpr/ppermute | solution.py:16
  51.7 7.1 %collective-permute-start.1 = (bf16[256,2,128]{2,0,1:T(8,128)(2,1)}, bf16[256,2,128]{2,0,1:T(8,128)(2,1)S(1)}, u32[]{:S(2)}, u32[]{:S(2)}) collective-permute-start(bf16[256,2,128]{2,0,1:T(8,128)(2,1)} %get-tuple-element.301), channel_id=1, source_target_pairs={{0,4},{4,8},{8,12},{12,16},{16,20},{20,24},{24,28},{1,5},{5,9},{9,... | collective-permute-start | bytes 393224 | tf_op jit(solution)/shard_map/while/body/eval_jaxpr/ppermute | solution.py:16
  56.1 3.4 %copy-start.1 = (f32[2,2,256,128]{3,2,1,0:T(8,128)S(1)}, f32[2,2,256,128]{3,2,1,0:T(8,128)}, u32[]{:S(2)}) copy-start(f32[2,2,256,128]{3,2,1,0:T(8,128)} %get-tuple-element.298) | copy-start | bytes 1572868 | tf_op jit(solution)/shard_map/while
  59.9 0.8 copy-start.2
  60.7 7.9 %collective-permute-start = (bf16[256,2,128]{2,0,1:T(8,128)(2,1)S(1)}, bf16[256,2,128]{2,0,1:T(8,128)(2,1)S(1)}, u32[]{:S(2)}, u32[]{:S(2)}) collective-permute-start(bf16[256,2,128]{2,0,1:T(8,128)(2,1)S(1)} %get-tuple-element.300), channel_id=1, source_target_pairs={{0,4},{4,8},{8,12},{12,16},{16,20},{20,24},{24,28},{1,5},{5,9},{9,... | collective-permute-start | bytes 393224 | tf_op jit(solution)/shard_map/while/body/eval_jaxpr/ppermute | solution.py:16
  65.0 6.3 %collective-permute-start.1 = (bf16[256,2,128]{2,0,1:T(8,128)(2,1)}, bf16[256,2,128]{2,0,1:T(8,128)(2,1)S(1)}, u32[]{:S(2)}, u32[]{:S(2)}) collective-permute-start(bf16[256,2,128]{2,0,1:T(8,128)(2,1)} %get-tuple-element.301), channel_id=1, source_target_pairs={{0,4},{4,8},{8,12},{12,16},{16,20},{20,24},{24,28},{1,5},{5,9},{9,... | collective-permute-start | bytes 393224 | tf_op jit(solution)/shard_map/while/body/eval_jaxpr/ppermute | solution.py:16
  68.5 3.4 %copy-start.1 = (f32[2,2,256,128]{3,2,1,0:T(8,128)S(1)}, f32[2,2,256,128]{3,2,1,0:T(8,128)}, u32[]{:S(2)}) copy-start(f32[2,2,256,128]{3,2,1,0:T(8,128)} %get-tuple-element.298) | copy-start | bytes 1572868 | tf_op jit(solution)/shard_map/while
  72.3 0.8 copy-start.2
  73.1 8.7 %collective-permute-start = (bf16[256,2,128]{2,0,1:T(8,128)(2,1)S(1)}, bf16[256,2,128]{2,0,1:T(8,128)(2,1)S(1)}, u32[]{:S(2)}, u32[]{:S(2)}) collective-permute-start(bf16[256,2,128]{2,0,1:T(8,128)(2,1)S(1)} %get-tuple-element.300), channel_id=1, source_target_pairs={{0,4},{4,8},{8,12},{12,16},{16,20},{20,24},{24,28},{1,5},{5,9},{9,... | collective-permute-start | bytes 393224 | tf_op jit(solution)/shard_map/while/body/eval_jaxpr/ppermute | solution.py:16
  77.4 7.1 %collective-permute-start.1 = (bf16[256,2,128]{2,0,1:T(8,128)(2,1)}, bf16[256,2,128]{2,0,1:T(8,128)(2,1)S(1)}, u32[]{:S(2)}, u32[]{:S(2)}) collective-permute-start(bf16[256,2,128]{2,0,1:T(8,128)(2,1)} %get-tuple-element.301), channel_id=1, source_target_pairs={{0,4},{4,8},{8,12},{12,16},{16,20},{20,24},{24,28},{1,5},{5,9},{9,... | collective-permute-start | bytes 393224 | tf_op jit(solution)/shard_map/while/body/eval_jaxpr/ppermute | solution.py:16
  81.7 3.4 %copy-start.1 = (f32[2,2,256,128]{3,2,1,0:T(8,128)S(1)}, f32[2,2,256,128]{3,2,1,0:T(8,128)}, u32[]{:S(2)}) copy-start(f32[2,2,256,128]{3,2,1,0:T(8,128)} %get-tuple-element.298) | copy-start | bytes 1572868 | tf_op jit(solution)/shard_map/while
  85.6 0.8 copy-start.2
  86.4 7.9 %collective-permute-start = (bf16[256,2,128]{2,0,1:T(8,128)(2,1)S(1)}, bf16[256,2,128]{2,0,1:T(8,128)(2,1)S(1)}, u32[]{:S(2)}, u32[]{:S(2)}) collective-permute-start(bf16[256,2,128]{2,0,1:T(8,128)(2,1)S(1)} %get-tuple-element.300), channel_id=1, source_target_pairs={{0,4},{4,8},{8,12},{12,16},{16,20},{20,24},{24,28},{1,5},{5,9},{9,... | collective-permute-start | bytes 393224 | tf_op jit(solution)/shard_map/while/body/eval_jaxpr/ppermute | solution.py:16
  90.6 6.3 %collective-permute-start.1 = (bf16[256,2,128]{2,0,1:T(8,128)(2,1)}, bf16[256,2,128]{2,0,1:T(8,128)(2,1)S(1)}, u32[]{:S(2)}, u32[]{:S(2)}) collective-permute-start(bf16[256,2,128]{2,0,1:T(8,128)(2,1)} %get-tuple-element.301), channel_id=1, source_target_pairs={{0,4},{4,8},{8,12},{12,16},{16,20},{20,24},{24,28},{1,5},{5,9},{9,... | collective-permute-start | bytes 393224 | tf_op jit(solution)/shard_map/while/body/eval_jaxpr/ppermute | solution.py:16
  94.1 3.4 %copy-start.1 = (f32[2,2,256,128]{3,2,1,0:T(8,128)S(1)}, f32[2,2,256,128]{3,2,1,0:T(8,128)}, u32[]{:S(2)}) copy-start(f32[2,2,256,128]{3,2,1,0:T(8,128)} %get-tuple-element.298) | copy-start | bytes 1572868 | tf_op jit(solution)/shard_map/while
  98.0 0.8 copy-start.2
  100.1 6.9 %collective-permute-start.2 = (bf16[256,4,128]{2,0,1:T(8,128)(2,1)S(1)}, bf16[256,4,128]{2,0,1:T(8,128)(2,1)}, u32[]{:S(2)}, u32[]{:S(2)}) collective-permute-start(bf16[256,4,128]{2,0,1:T(8,128)(2,1)S(1)} %bitcast.49), channel_id=1, source_target_pairs={{0,1},{1,2},{2,3},{3,0},{4,5},{5,6},{6,7},{7,4},{8,9},{9,10},{10,1... | collective-permute-start | bytes 786440 | tf_op jit(solution)/shard_map/ppermute | solution.py:108
  100.1 11.2 %collective-permute-start.3 = (bf16[256,4,128]{2,0,1:T(8,128)(2,1)S(1)}, bf16[256,4,128]{2,0,1:T(8,128)(2,1)}, u32[]{:S(2)}, u32[]{:S(2)}) collective-permute-start(bf16[256,4,128]{2,0,1:T(8,128)(2,1)S(1)} %bitcast.50), channel_id=1, source_target_pairs={{0,3},{1,0},{2,1},{3,2},{4,7},{5,4},{6,5},{7,6},{8,11},{9,8},{10,9... | collective-permute-start | bytes 786440 | tf_op jit(solution)/shard_map/ppermute | solution.py:113
  106.9 6.1 %collective-permute-start.4 = (bf16[256,4,128]{2,0,1:T(8,128)(2,1)}, bf16[256,4,128]{2,0,1:T(8,128)(2,1)}, u32[]{:S(2)}, u32[]{:S(2)}) collective-permute-start(bf16[256,4,128]{2,0,1:T(8,128)(2,1)} %collective-permute-done.2), channel_id=1, source_target_pairs={{0,1},{1,2},{2,3},{3,0},{4,5},{5,6},{6,7},{7,4},{8,9},{9,10},{10,1... | collective-permute-start | bytes 786440 | tf_op jit(solution)/shard_map/ppermute | solution.py:108
  113.0 13.1 %copy-start.4 = (bf16[256,768]{1,0:T(8,128)(2,1)S(1)}, bf16[256,768]{1,0:T(8,128)(2,1)}, u32[]{:S(2)}) copy-start(bf16[256,768]{1,0:T(8,128)(2,1)} %param.11) | copy-start | bytes 1179652
